TPU v7x, 512 devices: a whole 4x4x16 slice. The times are simulated.
512 devices in a mesh: walker: 32 (over z, y_lo), orb: 16 (over x, y_hi, core).
Axes of the slice: x: 4, y: 4 (y_hi: 2, y_lo: 2; y = y_hi * 2 + y_lo), z: 16, core: 2. Of those that a mesh axis runs over, the one named last changes fastest.
Arguments:
- tile_index: int32 [32768], P('walker'), may hold values from 0 to 63
- weights: bfloat16 [32768, 64], P('walker'), may hold values from -0.75 to 0.75
- electron: int32 [32768], P('walker'), may hold values from 0 to 767
- strength: float32 [32768], P('walker'), may hold values from -1.5 to 1.5
- spline_table: bfloat16 [4096, 4096], P(None, 'orb'), may hold values from -6 to 6
- rotation: bfloat16 [4096, 768], P('orb'), may hold values from -0.09375 to 0.09375
- inverse: bfloat16 [32, 768, 768], P('walker', 'orb'), may hold values from -0.21875 to 0.21875
Outputs:
- ratios: float32 [32768], P(('walker', 'orb'))
- gradient: float32 [4096, 768], P('orb')
All inputs are finite; a program needn't handle non-finite values.
Results may differ from a plain program's by a relative error of at most 0.0042.
Values may be sent and summed in bfloat16 or wider, within the bound.
No kernel may reach another device: no remote copies, remote signals or barrier semaphores. Data moves between devices by JAX's collectives and lax.ppermute only.
A program may use at most 64 MiB of HBM per device.

v0:
```python
import jax
import jax.numpy as jnp
from jax import lax
from jax.sharding import PartitionSpec as P


def body(tile_index, weights, electron, strength, spline_table, rotation, inverse):
    points = tile_index.shape[0]
    coeffs = weights.shape[1]
    tiles_count = spline_table.shape[0] // coeffs
    electrons = inverse.shape[2]
    inverse_full = lax.all_gather(inverse[0], "orb", axis=0, tiled=True)
    onehot = (tile_index[:, None] == jnp.arange(tiles_count, dtype=jnp.int32)[None, :]).astype(
        jnp.bfloat16
    )
    stencil_matrix = (onehot[:, :, None] * weights[:, None, :]).reshape(
        points, tiles_count * coeffs
    )
    orbital_values = jnp.dot(
        stencil_matrix, spline_table, preferred_element_type=jnp.float32
    ).astype(jnp.bfloat16)
    pick = (electron[:, None] == jnp.arange(electrons, dtype=jnp.int32)[None, :]).astype(
        jnp.bfloat16
    )
    columns = lax.dot_general(
        pick, inverse_full, (((1,), (1,)), ((), ())), preferred_element_type=jnp.float32
    )
    adjoint = (columns * strength[:, None]).astype(jnp.bfloat16)
    local_gradient = lax.dot_general(
        orbital_values, adjoint, (((0,), (0,)), ((), ())), preferred_element_type=jnp.float32
    )
    rotated_columns = lax.dot_general(
        columns.astype(jnp.bfloat16),
        rotation,
        (((1,), (1,)), ((), ())),
        preferred_element_type=jnp.float32,
    )
    partial_ratio = jnp.sum(orbital_values.astype(jnp.float32) * rotated_columns, axis=1)
    ratios = lax.psum_scatter(partial_ratio, "orb", scatter_dimension=0, tiled=True)
    gradient = lax.psum(local_gradient, "walker")
    return (ratios, gradient)


def solution(mesh):
    in_specs = (
        P("walker"),
        P("walker", None),
        P("walker"),
        P("walker"),
        P(None, "orb"),
        P("orb", None),
        P("walker", "orb", None),
    )
    out_specs = (P(("walker", "orb")), P("orb", None))
    return jax.shard_map(body, mesh=mesh, in_specs=in_specs, out_specs=out_specs, check_vma=False)
```

profile of v0, /device:TPU:4, one launch (start us, length us, event | category | flops | bytes accessed | tf_op | source)
XLA Modules:
  0.0 357.1 jit_solution(11248412728367267794)
XLA Ops:
  7.2 0.0 copy-start
  7.2 0.0 all-gather.3.cloned.1.call-start
  7.2 0.7 all-gather.3.cloned.1.call-update
  7.9 0.0 all-reduce.3.cloned.1.call-start
  8.0 0.7 fusion.13
  8.7 1.5 broadcast_multiply_fusion
  10.1 0.0 copy-done
  10.1 0.0 copy-start.4
  10.2 2.4 convolution_convert_fusion
  12.6 0.0 copy-start.3
  12.6 62.3 %all-gather.3.cloned.1.call-done = bf16[1,768,768]{2,1,0:T(8,128)(2,1)} async-done(((bf16[1,48,768]{2,1,0:T(8,128)(2,1)}), bf16[1,768,768]{2,1,0:T(8,128)(2,1)}) %all-gather.3.cloned.1.call-update) | async-done | bytes 1179664 | tf_op jit(solution)/shard_map/all_gather | solution.py:12
  74.9 0.0 copy-done.4
  74.9 2.8 fusion
  77.7 0.0 copy-start.1
  77.7 1.6 copy-done.1
  79.4 0.0 copy-done.3
  79.4 0.0 copy-start.2
  79.4 1.6 fusion.1
  81.0 0.0 all-reduce.3.cloned.1.call-update
  81.0 1.3 dynamic-slice
  82.9 0.0 copy-done.2
  82.9 2.5 fusion.9
  85.5 30.2 %all-reduce = f32[1024]{0:T(1024)S(1)} all-reduce(f32[1024]{0:T(1024)S(1)} %fusion.9), channel_id=3, replica_groups=mesh['walker'=32,'orb'=16] {'orb'}, use_global_device_ids=true, to_apply=%region_1.0.clone | all-reduce | flops 1024 | bytes 8192
  115.7 0.6 dynamic-slice.1
  116.3 232.0 %all-reduce.3.cloned.1.call-done = f32[256,768]{1,0:T(8,128)} async-done(((f32[256,768]{1,0:T(8,128)}), f32[256,768]{1,0:T(8,128)}) %all-reduce.3.cloned.1.call-update) | async-done | bytes 786448 | tf_op jit(solution)/shard_map/psum | solution.py:40
  348.2 2.1 copy.11
Async XLA Ops:
  7.2 3.0 copy-start
  7.2 67.7 %all-gather.3.cloned.1.call-start = ((), (), s32[]{:S(2)}) async-start(), calls=%async_computation.1 | async-start | bytes 1253376 | tf_op jit(solution)/shard_map/all_gather | solution.py:12
  7.9 340.3 %all-reduce.3.cloned.1.call-start = ((), (), s32[]{:S(2)}) async-start(), calls=%async_computation | async-start | bytes 1572864 | tf_op jit(solution)/shard_map/psum | solution.py:40
  10.1 64.8 %copy-start.4 = (s32[1024]{0:T(1024)S(1)}, s32[1024]{0:T(1024)}, u32[]{:S(2)}) copy-start(s32[1024]{0:T(1024)} %param.9) | copy-start | bytes 12292
  12.6 66.8 %copy-start.3 = (f32[1024]{0:T(1024)S(1)}, f32[1024]{0:T(1024)}, u32[]{:S(2)}) copy-start(f32[1024]{0:T(1024)} %param.10) | copy-start | bytes 12292
  77.7 1.7 copy-start.1
  79.4 3.6 copy-start.2
Sparse Core Ops, SparseCore 0:
  11.3 63.6 all-gather.2
  81.1 267.0 all-reduce.2
where the time goes:
time: 357 us
  waiting for transfers between devices  295 us (83%)
  blocking collectives  30.2 us (8%)
  between operations  14.8 us (4%)
  matrix products  9.31 us (3%)
  local copies, waits for them, and re-layouts  5.59 us (2%)
    psum x1, waiting for transfers between devices, body(): gradient = lax.psum(local_gradient, 'walker')  232 us
    all_gather x1, waiting for transfers between devices, body(): inverse_full = lax.all_gather(inverse[0], 'orb', axis=0, tiled=True)  62.3 us
    unnamed x1, blocking collectives  30.2 us
  transfers between devices with their start and end apart: 2, of which 2 were waited for; matrix products, arithmetic and copies ran while one was open for 3% of the time, Pallas kernels for 0%

commit v1 on v0

--- a/solution.py
+++ b/solution.py
@@ -9,7 +9,9 @@
     coeffs = weights.shape[1]
     tiles_count = spline_table.shape[0] // coeffs
     electrons = inverse.shape[2]
-    inverse_full = lax.all_gather(inverse[0], "orb", axis=0, tiled=True)
+    inverse_full = jnp.concatenate(
+        lax.all_to_all(jnp.stack([inverse[0]] * lax.axis_size("orb")), "orb", 0, 0), axis=0
+    )
     onehot = (tile_index[:, None] == jnp.arange(tiles_count, dtype=jnp.int32)[None, :]).astype(
         jnp.bfloat16
     )

time: 357 us -> 319 us (0.89)
  waiting for transfers between devices: 295 us -> 247 us
  starting transfers between devices: 0.08 us -> 10.1 us
    all_gather x1 -> x0, waiting for transfers between devices: 62.3 us -> none  [body(): inverse_full = lax.all_gather(inverse[0], 'orb', axis=0, tiled=True)]
    all_to_all x0 -> x1, waiting for transfers between devices: none -> 14.2 us  [body(): lax.all_to_all(jnp.stack([inverse[0]] * lax.axis_size('orb')), 'orb', 0, 0)]
    all_to_all x0 -> x1, starting transfers between devices: none -> 10 us  [body(): lax.all_to_all(jnp.stack([inverse[0]] * lax.axis_size('orb')), 'orb', 0, 0)]
  transfers between devices with their start and end apart: 2 -> 2, of which waited for: 2 -> 2; matrix products, arithmetic and copies ran while one was open for 3% -> 2% of each run, Pallas kernels for 0% -> 0%
where the time goes in v1:
time: 319 us; the launch traced here: 318 us
  waiting for transfers between devices  247 us (77%)
  blocking collectives  28.9 us (9%)
  between operations  14.8 us (5%)
  starting transfers between devices  10.1 us (3%)
  matrix products  9.33 us (3%)
  local copies, waits for them, and re-layouts  7.74 us (2%)
    psum x1, waiting for transfers between devices, body(): gradient = lax.psum(local_gradient, 'walker')  233 us
    unnamed x1, blocking collectives  28.9 us
    all_to_all x1, waiting for transfers between devices, body(): lax.all_to_all(jnp.stack([inverse[0]] * lax.axis_size('orb')), 'orb', 0, 0)  14.2 us
    all_to_all x1, starting transfers between devices, body(): lax.all_to_all(jnp.stack([inverse[0]] * lax.axis_size('orb')), 'orb', 0, 0)  10 us
  transfers between devices with their start and end apart: 2, of which 2 were waited for; matrix products, arithmetic and copies ran while one was open for 2% of the time, Pallas kernels for 0%

profile of v1, /device:TPU:4, one launch (start us, length us, event | category | flops | bytes accessed | tf_op | source)
XLA Modules:
  0.0 318.2 jit_solution(17777520003012769134)
XLA Ops:
  7.2 0.0 copy-start
  7.2 0.0 copy-start.5
  7.2 0.0 copy-start.3
  7.2 2.1 stack.3
  9.3 10.0 %all-to-all-start = ((bf16[16,48,768]{2,1,0:T(8,128)(2,1)}), bf16[16,48,768]{2,1,0:T(8,128)(2,1)}, u32[]{:S(2)}, u32[]{:S(2)}) async-start(bf16[16,48,768]{2,1,0:T(8,128)(2,1)} %stack.3), calls=%async_computation | async-start | bytes 2359296 | tf_op jit(solution)/shard_map/all_to_all | solution.py:13
  19.4 0.0 all-reduce.3.cloned.1.call-start
  19.4 0.0 copy-done.5
  19.5 0.0 copy-done.3
  19.5 0.6 broadcast_multiply_fusion
  20.0 0.0 copy-done
  20.0 0.0 copy-start.6
  20.0 2.4 convolution_convert_fusion
  22.4 14.2 %all-to-all-done = bf16[16,48,768]{2,1,0:T(8,128)(2,1)} async-done(((bf16[16,48,768]{2,1,0:T(8,128)(2,1)}), bf16[16,48,768]{2,1,0:T(8,128)(2,1)}, u32[]{:S(2)}, u32[]{:S(2)}) %all-to-all-start) | async-done | bytes 1179680 | tf_op jit(solution)/shard_map/all_to_all | solution.py:13
  36.6 0.0 copy-done.6
  36.6 0.0 copy-start.4
  36.6 2.8 fusion
  39.5 0.0 copy-start.1
  39.5 1.6 copy-done.1
  41.1 0.0 copy-done.4
  41.1 0.0 copy-start.2
  41.1 1.6 fusion.1
  42.7 0.0 all-reduce.3.cloned.1.call-update
  42.8 1.3 dynamic-slice
  44.7 0.0 copy-done.2
  44.7 2.5 fusion.9
  47.2 28.9 %all-reduce = f32[1024]{0:T(1024)S(1)} all-reduce(f32[1024]{0:T(1024)S(1)} %fusion.9), channel_id=2, replica_groups=mesh['walker'=32,'orb'=16] {'orb'}, use_global_device_ids=true, to_apply=%region_1.0.clone | all-reduce | flops 1024 | bytes 8192
  76.1 0.6 dynamic-slice.1
  76.7 232.6 %all-reduce.3.cloned.1.call-done = f32[256,768]{1,0:T(8,128)} async-done(((f32[256,768]{1,0:T(8,128)}), f32[256,768]{1,0:T(8,128)}) %all-reduce.3.cloned.1.call-update) | async-done | bytes 786448 | tf_op jit(solution)/shard_map/psum | solution.py:42
  309.3 2.1 copy.11
  (1 shorter events, 0.0 us)
Async XLA Ops:
  7.2 12.9 %copy-start = (bf16[4096,256]{1,0:T(8,128)(2,1)S(1)}, bf16[4096,256]{1,0:T(8,128)(2,1)}, u32[]{:S(2)}) copy-start(bf16[4096,256]{1,0:T(8,128)(2,1)} %param.11) | copy-start | bytes 6291460
  7.2 12.2 %copy-start.5 = (s32[1024]{0:T(1024)S(1)}, s32[1024]{0:T(1024)}, u32[]{:S(2)}) copy-start(s32[1024]{0:T(1024)} %param.7) | copy-start | bytes 12292
  7.2 12.3 %copy-start.3 = (bf16[1024,64]{0,1:T(8,128)(2,1)S(1)}, bf16[1024,64]{0,1:T(8,128)(2,1)}, u32[]{:S(2)}) copy-start(bf16[1024,64]{0,1:T(8,128)(2,1)} %param.8) | copy-start | bytes 393220
  9.3 27.3 %all-to-all-start = ((bf16[16,48,768]{2,1,0:T(8,128)(2,1)}), bf16[16,48,768]{2,1,0:T(8,128)(2,1)}, u32[]{:S(2)}, u32[]{:S(2)}) async-start(bf16[16,48,768]{2,1,0:T(8,128)(2,1)} %stack.3), calls=%async_computation | async-start | bytes 2359296 | tf_op jit(solution)/shard_map/all_to_all | solution.py:13
  19.4 289.9 %all-reduce.3.cloned.1.call-start = ((), (), s32[]{:S(2)}) async-start(), calls=%async_computation.1 | async-start | bytes 1572864 | tf_op jit(solution)/shard_map/psum | solution.py:42
  20.0 16.6 %copy-start.6 = (s32[1024]{0:T(1024)S(1)}, s32[1024]{0:T(1024)}, u32[]{:S(2)}) copy-start(s32[1024]{0:T(1024)} %param.9) | copy-start | bytes 12292
  36.6 4.5 %copy-start.4 = (f32[1024]{0:T(1024)S(1)}, f32[1024]{0:T(1024)}, u32[]{:S(2)}) copy-start(f32[1024]{0:T(1024)} %param.10) | copy-start | bytes 12292
  39.5 1.6 copy-start.1
  41.1 3.6 %copy-start.2 = (bf16[256,768]{1,0:T(8,128)(2,1)S(1)}, bf16[256,768]{1,0:T(8,128)(2,1)}, u32[]{:S(2)}) copy-start(bf16[256,768]{1,0:T(8,128)(2,1)} %param.12) | copy-start | bytes 1179652
Sparse Core Ops, SparseCore 0:
  42.9 266.3 all-reduce.2
